TPU v7x, 256 devices: a whole 4x4x8 slice. The times are simulated.
256 devices in a mesh: mem: 4 (over x), col: 64 (over y, z, core).
Axes of the slice: x: 4, y: 4, z: 8, core: 2. Of those that a mesh axis runs over, the one named last changes fastest.
Arguments:
- perturbations: bfloat16 [32, 256, 256, 128], P('mem', 'col'), may hold values from -4 to 4
- static_root: float32 [128, 128], replicated, may hold values from -0.5 to 1.5
- obs_jacobian: float32 [128, 128], replicated, may hold values from -0.5 to 0.5
- innovations: float32 [16384, 128], P('col'), may hold values from -6 to 6
- obs_weights: float32 [128], replicated, may hold values from 0.2 to 2
- length_scale: float32 [256, 256], P('col'), may hold values from 0.05 to 0.24
- obs_owner: int32 [16384, 1], P('col'), may hold values from 0 to 63; in each aligned block of 256 rows (0 to 255, 256 to 511, ...) at most 8 rows name the same one
- obs_cell: int32 [16384], P('col'), may hold values from 0 to 1023
- obs_count: int32 [64], P('col'), may hold values from 128 to 256, as said below
Outputs:
- increment: float32 [256, 256, 128], P('col', 'mem')
- control_static: float32 [256, 256, 128], P('col', 'mem')
- control_ensemble: float32 [32, 256, 256], P('mem', 'col')
Inputs may be any that keep to these rules, and one draw needn't show every extreme that they name: `obs_owner`: each holder's 256 rows name any one column block at most 8 times. `obs_count`: rows at or past a holder's count are padding and are ignored; at least one holder is full. `obs_cell`: the column within the owner's block, numbered y * 256 + x, where y is its grid row within the block (0 to 3).
All inputs are finite; a program needn't handle non-finite values.
Results may differ from a plain program's by a relative error of at most 0.004.
Values may be sent and summed in bfloat16 or wider, within the bound.
No kernel may reach another device: no remote copies, remote signals or barrier semaphores. Data moves between devices by JAX's collectives and lax.ppermute only.
A program may use at most 64 MiB of HBM per device.

v0:
```python
import jax
import jax.numpy as jnp
from jax import lax
from jax.sharding import PartitionSpec as P

NSWEEP = 4
ITERS = 2


def extended(block, sides, width):
    for axis, dim in sides:
        count = lax.axis_size(axis)
        forward = [(i, i + 1) for i in range(count - 1)]
        backward = [(target, source) for source, target in forward]
        low = lax.ppermute(
            lax.slice_in_dim(block, block.shape[dim] - width, None, axis=dim), axis, forward
        )
        high = lax.ppermute(lax.slice_in_dim(block, 0, width, axis=dim), axis, backward)
        block = jnp.concatenate([low, block, high], axis=dim)
    return block


def face_coefficients(length_scale):
    rimmed = extended(length_scale, (("col", 0),), 1)
    padded = jnp.pad(rimmed, ((0, 0), (1, 1)))
    return (
        jnp.sqrt(length_scale * padded[:-2, 1:-1]),
        jnp.sqrt(length_scale * padded[2:, 1:-1]),
        jnp.sqrt(length_scale * padded[1:-1, :-2]),
        jnp.sqrt(length_scale * padded[1:-1, 2:]),
    )


def sweeps(values, coeffs):
    face_up, face_down, face_left, face_right = coeffs
    for sweep_step in range(NSWEEP):
        rimmed = extended(values, (("col", 1),), 1)
        padded = jnp.pad(rimmed, ((0, 0), (0, 0), (1, 1)))
        centre = values
        values = (
            centre
            + face_up * (padded[:, :-2, 1:-1] - centre)
            + face_down * (padded[:, 2:, 1:-1] - centre)
            + face_left * (padded[:, 1:-1, :-2] - centre)
            + face_right * (padded[:, 1:-1, 2:] - centre)
        )
    return values


def local_inner(first, second):
    return jnp.sum(first[0] * second[0]) + jnp.sum(first[1] * second[1])


def shards(
    perturbations,
    static_root,
    obs_jacobian,
    innovations,
    obs_weights,
    length_scale,
    obs_owner,
    obs_cell,
    obs_count,
):
    members, rows_here, columns, features = perturbations.shape
    quarter = columns // lax.axis_size("mem")
    offset = lax.axis_index("mem") * quarter
    blocks = lax.axis_size("col")
    obs_dev, channels = innovations.shape
    capacity = max(2, 2 * obs_dev // blocks)
    total_slots = blocks * capacity
    coeffs = face_coefficients(length_scale)
    is_live = jnp.arange(obs_dev, dtype=jnp.int32) < obs_count[0]
    owner_ids = obs_owner[:, 0]
    onehot = (
        (owner_ids[:, None] == jnp.arange(blocks, dtype=jnp.int32)[None, :]) & is_live[:, None]
    ).astype(jnp.int32)
    slot_rank = jnp.sum((jnp.cumsum(onehot, axis=0) - onehot) * onehot, axis=1)
    slot_ids = jnp.where(is_live, owner_ids * capacity + slot_rank, total_slots)
    send_values = (
        jnp.zeros((total_slots, channels), jnp.float32).at[slot_ids].set(innovations, mode="drop")
    )
    send_cells = jnp.zeros((total_slots,), jnp.int32).at[slot_ids].set(obs_cell, mode="drop")
    send_marks = jnp.zeros((total_slots,), jnp.float32).at[slot_ids].set(1.0, mode="drop")
    got_values, got_cells, got_marks = (
        lax.all_to_all(
            send_values.reshape(blocks, capacity, channels),
            "col",
            split_axis=0,
            concat_axis=0,
            tiled=True,
        ),
        lax.all_to_all(
            send_cells.reshape(blocks, capacity), "col", split_axis=0, concat_axis=0, tiled=True
        ),
        lax.all_to_all(
            send_marks.reshape(blocks, capacity), "col", split_axis=0, concat_axis=0, tiled=True
        ),
    )
    got_values = got_values.reshape(total_slots, channels)
    got_cells = got_cells.reshape(total_slots)
    got_marks = got_marks.reshape(total_slots)
    obs_index = got_cells
    obs_gain = got_marks[:, None] * obs_weights[None, :]

    def spread_back(weighted):
        back = jnp.dot(weighted, obs_jacobian.T, precision=lax.Precision.HIGHEST)
        grid = jnp.zeros((rows_here * columns, features), jnp.float32).at[obs_index].add(back)
        return grid.reshape(rows_here, columns, features)

    def adjoint_map(gradient):
        own_gradient = lax.dynamic_slice_in_dim(gradient, offset, quarter, 1)
        rounded = gradient.astype(jnp.bfloat16)
        static = jnp.dot(
            own_gradient.reshape(rows_here * quarter, features),
            static_root.T,
            precision=lax.Precision.HIGHEST,
        ).reshape(rows_here, quarter, features)
        projected = jnp.einsum(
            "kyxf,yxf->kyx", perturbations, rounded, preferred_element_type=jnp.float32
        )
        return (static, sweeps(projected, coeffs))

    residual = adjoint_map(spread_back(obs_gain * got_values))
    direction = residual
    state = (jnp.zeros_like(residual[0]), jnp.zeros_like(residual[1]))
    increment = jnp.zeros((rows_here, quarter, features), jnp.float32)
    norm_now = lax.psum(local_inner(residual, residual), ("mem", "col"))
    for iteration in range(ITERS):
        smoothed = sweeps(direction[1], coeffs).astype(jnp.bfloat16)
        partial_sum = jnp.einsum(
            "kyxf,kyx->yxf", perturbations, smoothed, preferred_element_type=jnp.float32
        )
        forward_static = jnp.dot(
            direction[0].reshape(rows_here * quarter, features),
            static_root,
            precision=lax.Precision.HIGHEST,
        ).reshape(rows_here, quarter, features)
        own_slice = lax.dynamic_slice_in_dim(partial_sum, offset, quarter, 1) + forward_static
        partial_sum = lax.dynamic_update_slice_in_dim(partial_sum, own_slice, offset, 1)
        image_part = lax.psum(partial_sum, "mem")
        own_image = lax.dynamic_slice_in_dim(image_part, offset, quarter, 1)
        image_part, own_image = (image_part, own_image)
        gathered = image_part.reshape(rows_here * columns, features)[obs_index]
        model_obs = jnp.dot(gathered, obs_jacobian, precision=lax.Precision.HIGHEST)
        adj_static, adj_ensemble = adjoint_map(spread_back(obs_gain * model_obs))
        image = (direction[0] + adj_static, direction[1] + adj_ensemble)
        step = norm_now / lax.psum(local_inner(direction, image), ("mem", "col"))
        residual = (residual[0] - step * image[0], residual[1] - step * image[1])
        norm_next = lax.psum(local_inner(residual, residual), ("mem", "col"))
        state = (state[0] + step * direction[0], state[1] + step * direction[1])
        increment = increment + step * own_image
        ratio = norm_next / norm_now
        direction = (residual[0] + ratio * direction[0], residual[1] + ratio * direction[1])
        norm_now = norm_next
    return (increment, state[0], state[1])


def solution(mesh):
    placed = (
        P("mem", "col", None, None),
        P(),
        P(),
        P("col", None),
        P(),
        P("col", None),
        P("col", None),
        P("col"),
        P("col"),
    )
    return jax.shard_map(
        shards,
        mesh=mesh,
        in_specs=placed,
        out_specs=(P("col", "mem", None), P("col", "mem", None), P("mem", "col", None)),
        check_vma=False,
    )
```

profile of v0, /device:TPU:1, one launch (start us, length us, event | category | flops | bytes accessed | tf_op | source)
XLA Modules:
  0.0 626.9 jit_solution(7078985824332760388)
XLA Ops:
  13.3 13.1 %all-to-all-start = ((s32[64,1,8]{2,1,0:T(1,128)}), s32[64,1,8]{2,1,0:T(1,128)S(1)}, u32[]{:S(2)}, u32[]{:S(2)}) async-start(s32[64,1,8]{2,1,0:T(1,128)} %bitcast.6), calls=%async_computation | async-start | bytes 65536 | tf_op jit(solution)/shard_map/all_to_all | solution.py:93
  28.5 7.1 %all-to-all-done = s32[64,1,8]{2,1,0:T(1,128)S(1)} async-done(((s32[64,1,8]{2,1,0:T(1,128)}), s32[64,1,8]{2,1,0:T(1,128)S(1)}, u32[]{:S(2)}, u32[]{:S(2)}) %all-to-all-start) | async-done | bytes 2080 | tf_op jit(solution)/shard_map/all_to_all | solution.py:93
  35.7 4.7 all-to-all-start.1
  42.5 7.2 %all-to-all-done.1 = f32[64,1,8]{2,1,0:T(1,128)S(1)} async-done(((f32[64,1,8]{2,1,0:T(1,128)}), f32[64,1,8]{2,1,0:T(1,128)S(1)}, u32[]{:S(2)}, u32[]{:S(2)}) %all-to-all-start.1) | async-done | bytes 2080 | tf_op jit(solution)/shard_map/all_to_all | solution.py:96
  49.7 4.7 all-to-all-start.2
  55.3 3.5 collective-permute-start
  60.7 3.2 collective-permute-done.2
  68.7 2.4 scatter_custom_fusion.3
  73.1 3.3 collective-permute-start.1
  78.4 2.9 collective-permute-done.3
  86.0 2.6 collective-permute-done.5
  93.2 2.9 collective-permute-done.7
  98.3 2.4 collective-permute-start.9
  100.7 4.8 collective-permute-done.9
  107.9 2.4 collective-permute-start.11
  110.3 3.8 collective-permute-done.11
  118.7 3.8 collective-permute-done.13
  124.7 2.4 collective-permute-start.15
  128.0 2.9 collective-permute-done.15
  133.1 2.4 collective-permute-start.17
  136.4 2.9 collective-permute-done.17
  142.6 54.8 %all-reduce.25.cloned.1.call-done = f32[4,256,128]{2,1,0:T(8,128)} async-done(((f32[4,256,128]{2,1,0:T(8,128)}), f32[4,256,128]{2,1,0:T(8,128)}) %all-reduce.25.cloned.1.call-update) | async-done | bytes 524304 | tf_op jit(solution)/shard_map/psum | solution.py:141
  200.2 2.4 scatter_custom_fusion.4
  202.7 2.4 fusion.6
  206.3 6.9 %collective-permute-start.18 = (f32[8,1,256]{2,1,0:T(1,128)S(1)}, f32[8,1,256]{2,1,0:T(1,128)S(1)}, u32[]{:S(2)}, u32[]{:S(2)}) collective-permute-start(f32[8,1,256]{2,1,0:T(1,128)S(1)} %get-tuple-element.30), channel_id=1, source_target_pairs={{0,1},{1,2},{2,3},{3,4},{4,5},{5,6},{6,7},{7,8},{8,9},{9,10},{10,1... | collective-permute-start | bytes 24584 | tf_op jit(solution)/shard_map/ppermute | solution.py:15
  215.1 3.0 collective-permute-done.19
  220.4 2.4 collective-permute-start.21
  222.8 2.6 collective-permute-done.21
  227.6 2.4 collective-permute-start.23
  230.0 2.6 collective-permute-done.23
  238.0 3.9 collective-permute-done.25
  245.4 80.6 %all-reduce.21 = (f32[]{:T(128)}, f32[]{:T(128)}) all-reduce(f32[]{:T(128)S(6)} %add.401, f32[]{:T(128)S(6)} %add.437), channel_id=1, replica_groups=mesh['mem'=4,'col'=64] {'mem','col'}, use_global_device_ids=true, to_apply=%region_9.10 | all-reduce | flops 2 | bytes 16 | tf_op jit(solution)/shard_map/psum | solution.py:128
  329.9 73.2 %psum.45 = f32[]{:T(128)} all-reduce(f32[]{:T(128)S(6)} %add.438), channel_id=1, replica_groups=mesh['mem'=4,'col'=64] {'mem','col'}, use_global_device_ids=true, to_apply=%region_17.18 | all-reduce | flops 1 | bytes 8 | tf_op jit(solution)/shard_map/psum | solution.py:150
  404.4 4.2 collective-permute-start.26
  410.8 2.8 collective-permute-done.27
  418.3 2.6 collective-permute-done.29
  425.5 2.6 collective-permute-done.31
  432.7 2.6 collective-permute-done.33
  436.6 2.8 fusion.4
  440.4 48.7 %all-reduce.27.cloned.1.call-done = f32[4,256,128]{2,1,0:T(8,128)} async-done(((f32[4,256,128]{2,1,0:T(8,128)}), f32[4,256,128]{2,1,0:T(8,128)}) %all-reduce.27.cloned.1.call-update) | async-done | bytes 524304 | tf_op jit(solution)/shard_map/psum | solution.py:141
  492.0 2.4 scatter_custom_fusion.5
  494.5 2.4 fusion.2
  498.1 6.8 %collective-permute-start.34 = (f32[8,1,256]{2,1,0:T(1,128)S(1)}, f32[8,1,256]{2,1,0:T(1,128)S(1)}, u32[]{:S(2)}, u32[]{:S(2)}) collective-permute-start(f32[8,1,256]{2,1,0:T(1,128)S(1)} %get-tuple-element.14), channel_id=1, source_target_pairs={{0,1},{1,2},{2,3},{3,4},{4,5},{5,6},{6,7},{7,8},{8,9},{9,10},{10,1... | collective-permute-start | bytes 24584 | tf_op jit(solution)/shard_map/ppermute | solution.py:15
  506.9 3.0 collective-permute-done.35
  514.5 2.6 collective-permute-done.37
  521.7 2.6 collective-permute-done.39
  529.8 4.0 collective-permute-done.41
  535.9 80.6 %psum.47 = f32[]{:T(128)} all-reduce(f32[]{:T(128)S(6)} %add.476), channel_id=1, replica_groups=mesh['mem'=4,'col'=64] {'mem','col'}, use_global_device_ids=true, to_apply=%region_22.23 | all-reduce | flops 1 | bytes 8 | tf_op jit(solution)/shard_map/psum | solution.py:148
  (188 shorter events, 108.7 us)
Async XLA Ops:
  7.2 64.0 %copy-start = (bf16[8,4,256,128]{3,2,1,0:T(8,128)(2,1)S(1)}, bf16[8,4,256,128]{3,2,1,0:T(8,128)(2,1)}, u32[]{:S(2)}) copy-start(bf16[8,4,256,128]{3,2,1,0:T(8,128)(2,1)} %param.9) | copy-start | bytes 6291460
  13.3 22.4 %all-to-all-start = ((s32[64,1,8]{2,1,0:T(1,128)}), s32[64,1,8]{2,1,0:T(1,128)S(1)}, u32[]{:S(2)}, u32[]{:S(2)}) async-start(s32[64,1,8]{2,1,0:T(1,128)} %bitcast.6), calls=%async_computation | async-start | bytes 65536 | tf_op jit(solution)/shard_map/all_to_all | solution.py:93
  35.7 14.1 %all-to-all-start.1 = ((f32[64,1,8]{2,1,0:T(1,128)}), f32[64,1,8]{2,1,0:T(1,128)S(1)}, u32[]{:S(2)}, u32[]{:S(2)}) async-start(f32[64,1,8]{2,1,0:T(1,128)} %bitcast.8), calls=%async_computation.1 | async-start | bytes 65536 | tf_op jit(solution)/shard_map/all_to_all | solution.py:96
  49.7 17.7 %all-to-all-start.2 = ((f32[64,8,128]{2,1,0:T(8,128)}), f32[64,8,128]{2,1,0:T(8,128)S(1)}, u32[]{:S(2)}, u32[]{:S(2)}) async-start(f32[64,8,128]{2,1,0:T(8,128)} %bitcast.9), calls=%async_computation.2 | async-start | bytes 524288 | tf_op jit(solution)/shard_map/all_to_all | solution.py:86
  54.4 142.9 %all-reduce.25.cloned.1.call-start = ((), (), s32[]{:S(2)}) async-start(), calls=%async_computation.3 | async-start | bytes 1048576 | tf_op jit(solution)/shard_map/psum | solution.py:141
  55.3 5.5 collective-permute-start
  58.8 5.2 collective-permute-start.2
  73.1 5.3 collective-permute-start.1
  76.4 5.0 collective-permute-start.3
  81.6 4.3 collective-permute-start.4
  83.6 5.0 collective-permute-start.5
  88.8 4.3 collective-permute-start.6
  90.8 5.2 collective-permute-start.7
  96.3 4.3 collective-permute-start.8
  98.3 7.2 %collective-permute-start.9 = (f32[8,1,256]{2,1,0:T(1,128)S(1)}, f32[8,1,256]{2,1,0:T(1,128)S(1)}, u32[]{:S(2)}, u32[]{:S(2)}) collective-permute-start(f32[8,1,256]{2,1,0:T(1,128)S(1)} %get-tuple-element.41), channel_id=1, source_target_pairs={{1,0},{2,1},{3,2},{4,3},{5,4},{6,5},{7,6},{8,7},{9,8},{10,9},{11,1... | collective-permute-start | bytes 24584 | tf_op jit(solution)/shard_map/ppermute | solution.py:18
  105.7 4.5 collective-permute-start.10
  107.9 6.2 collective-permute-start.11
  114.3 4.4 collective-permute-start.12
  116.3 6.2 collective-permute-start.13
  122.7 5.2 collective-permute-start.14
  124.7 6.2 collective-permute-start.15
  131.1 5.3 collective-permute-start.16
  133.1 6.2 collective-permute-start.17
  142.5 346.6 %all-reduce.27.cloned.1.call-start = ((), (), s32[]{:S(2)}) async-start(), calls=%async_computation.4 | async-start | bytes 1048576 | tf_op jit(solution)/shard_map/psum | solution.py:141
  206.3 8.8 %collective-permute-start.18 = (f32[8,1,256]{2,1,0:T(1,128)S(1)}, f32[8,1,256]{2,1,0:T(1,128)S(1)}, u32[]{:S(2)}, u32[]{:S(2)}) collective-permute-start(f32[8,1,256]{2,1,0:T(1,128)S(1)} %get-tuple-element.30), channel_id=1, source_target_pairs={{0,1},{1,2},{2,3},{3,4},{4,5},{5,6},{6,7},{7,8},{8,9},{9,10},{10,1... | collective-permute-start | bytes 24584 | tf_op jit(solution)/shard_map/ppermute | solution.py:15
  213.2 5.0 collective-permute-start.19
  218.4 4.3 collective-permute-start.20
  220.4 5.0 collective-permute-start.21
  225.6 4.3 collective-permute-start.22
  227.6 5.0 collective-permute-start.23
  232.8 5.2 collective-permute-start.24
  234.8 7.2 %collective-permute-start.25 = (f32[8,1,256]{2,1,0:T(1,128)S(1)}, f32[8,1,256]{2,1,0:T(1,128)S(1)}, u32[]{:S(2)}, u32[]{:S(2)}) collective-permute-start(f32[8,1,256]{2,1,0:T(1,128)S(1)} %get-tuple-element.25), channel_id=1, source_target_pairs={{1,0},{2,1},{3,2},{4,3},{5,4},{6,5},{7,6},{8,7},{9,8},{10,9},{11,1... | collective-permute-start | bytes 24584 | tf_op jit(solution)/shard_map/ppermute | solution.py:18
  404.4 6.4 %collective-permute-start.26 = (f32[8,1,256]{2,1,0:T(1,128)S(1)}, f32[8,1,256]{2,1,0:T(1,128)S(1)}, u32[]{:S(2)}, u32[]{:S(2)}) collective-permute-start(f32[8,1,256]{2,1,0:T(1,128)S(1)} %get-tuple-element.22), channel_id=1, source_target_pairs={{0,1},{1,2},{2,3},{3,4},{4,5},{5,6},{6,7},{7,8},{8,9},{9,10},{10,1... | collective-permute-start | bytes 24584 | tf_op jit(solution)/shard_map/ppermute | solution.py:15
  408.7 5.0 collective-permute-start.27
  413.9 4.3 collective-permute-start.28
  415.9 5.0 collective-permute-start.29
  421.1 4.3 collective-permute-start.30
  423.1 5.0 collective-permute-start.31
  428.3 4.3 collective-permute-start.32
  430.3 5.0 collective-permute-start.33
  498.1 8.8 %collective-permute-start.34 = (f32[8,1,256]{2,1,0:T(1,128)S(1)}, f32[8,1,256]{2,1,0:T(1,128)S(1)}, u32[]{:S(2)}, u32[]{:S(2)}) collective-permute-start(f32[8,1,256]{2,1,0:T(1,128)S(1)} %get-tuple-element.14), channel_id=1, source_target_pairs={{0,1},{1,2},{2,3},{3,4},{4,5},{5,6},{6,7},{7,8},{8,9},{9,10},{10,1... | collective-permute-start | bytes 24584 | tf_op jit(solution)/shard_map/ppermute | solution.py:15
  504.9 5.0 collective-permute-start.35
  510.2 4.3 collective-permute-start.36
  512.1 5.0 collective-permute-start.37
  517.4 4.3 collective-permute-start.38
  519.3 5.0 collective-permute-start.39
  524.6 5.2 collective-permute-start.40
  526.5 7.2 %collective-permute-start.41 = (f32[8,1,256]{2,1,0:T(1,128)S(1)}, f32[8,1,256]{2,1,0:T(1,128)S(1)}, u32[]{:S(2)}, u32[]{:S(2)}) collective-permute-start(f32[8,1,256]{2,1,0:T(1,128)S(1)} %get-tuple-element.9), channel_id=1, source_target_pairs={{1,0},{2,1},{3,2},{4,3},{5,4},{6,5},{7,6},{8,7},{9,8},{10,9},{11,1... | collective-permute-start | bytes 24584 | tf_op jit(solution)/shard_map/ppermute | solution.py:18
  (7 other events, 180.4 us)
Sparse Core Ops, SparseCore 0:
  142.7 54.6 all-reduce.24
  440.6 48.5 all-reduce.26
where the time goes:
time: 629 us; the launch traced here: 627 us
  blocking collectives  234 us (37%)
  waiting for transfers between devices  182 us (29%)
  starting transfers between devices  127 us (20%)
  between operations  25.3 us (4%)
  other arithmetic  22.1 us (4%)
  local copies, waits for them, and re-layouts  18.9 us (3%)
  matrix products  17.4 us (3%)
    psum x2, waiting for transfers between devices, shards(): image_part = lax.psum(partial_sum, 'mem')  104 us
    psum x1, blocking collectives, shards(): norm_now = lax.psum(local_inner(residual, residual), ('mem', 'col'))  80.6 us
    psum x1, blocking collectives, shards(): step = norm_now / lax.psum(local_inner(direction, image), ('mem', 'col'))  80.6 us
    psum x1, blocking collectives, shards(): norm_next = lax.psum(local_inner(residual, residual), ('mem', 'col'))  73.2 us
    ppermute x21, waiting for transfers between devices, extended(): lax.ppermute(lax.slice_in_dim(block, 0, width, axis=dim), axis, backward)  64.5 us
    ppermute x21, starting transfers between devices, extended(): lax.ppermute(lax.slice_in_dim(block, block.shape[dim] - width, None, axis...  56 us
    ppermute x21, starting transfers between devices, extended(): lax.ppermute(lax.slice_in_dim(block, 0, width, axis=dim), axis, backward)  47.9 us
    all_to_all x1, starting transfers between devices, shards(): lax.all_to_all(send_cells.reshape(blocks, capacity), 'col', split_axis=0,...  13.1 us
  transfers between devices with their start and end apart: 47, of which 25 were waited for; matrix products, arithmetic and copies ran while one was open for 2% of the time, Pallas kernels for 0%

commit v1 on v0

--- a/solution.py
+++ b/solution.py
@@ -138,7 +138,11 @@
         ).reshape(rows_here, quarter, features)
         own_slice = lax.dynamic_slice_in_dim(partial_sum, offset, quarter, 1) + forward_static
         partial_sum = lax.dynamic_update_slice_in_dim(partial_sum, own_slice, offset, 1)
-        image_part = lax.psum(partial_sum, "mem")
+        image_part = partial_sum
+        for hop in (1, 2):
+            image_part = image_part + lax.ppermute(
+                image_part, "mem", [(dev, dev ^ hop) for dev in range(4)]
+            )
         own_image = lax.dynamic_slice_in_dim(image_part, offset, quarter, 1)
         image_part, own_image = (image_part, own_image)
         gathered = image_part.reshape(rows_here * columns, features)[obs_index]

time: 629 us -> 587 us (0.933); the launches traced: 627 us -> 576 us
  waiting for transfers between devices: 182 us -> 126 us
  between operations: 25.3 us -> 11.9 us
  blocking collectives: 234 us -> 245 us
    psum x2 -> x0, waiting for transfers between devices: 104 us -> none  [shards(): image_part = lax.psum(partial_sum, 'mem')]
    ppermute x0 -> x4, waiting for transfers between devices: none -> 47.1 us  [shards(): lax.ppermute(image_part, 'mem', [(dev, dev ^ hop) for dev in range(4)])]
    ppermute x0 -> x4, starting transfers between devices: none -> 6.79 us  [shards(): lax.ppermute(image_part, 'mem', [(dev, dev ^ hop) for dev in range(4)])]
  transfers between devices with their start and end apart: 47 -> 49, of which waited for: 25 -> 27; matrix products, arithmetic and copies ran while one was open for 2% -> 2% of each run, Pallas kernels for 0% -> 0%
where the time goes in v1:
time: 587 us; the launch traced here: 576 us
  blocking collectives  245 us (42%)
  starting transfers between devices  130 us (22%)
  waiting for transfers between devices  126 us (21%)
  other arithmetic  26.2 us (4%)
  matrix products  19.9 us (3%)
  local copies, waits for them, and re-layouts  17.5 us (3%)
  between operations  11.9 us (2%)
    psum x1, blocking collectives, shards(): norm_now = lax.psum(local_inner(residual, residual), ('mem', 'col'))  86.9 us
    psum x1, blocking collectives, shards(): step = norm_now / lax.psum(local_inner(direction, image), ('mem', 'col'))  85.1 us
    psum x1, blocking collectives, shards(): norm_next = lax.psum(local_inner(residual, residual), ('mem', 'col'))  72.8 us
    ppermute x21, waiting for transfers between devices, extended(): lax.ppermute(lax.slice_in_dim(block, 0, width, axis=dim), axis, backward)  64.6 us
    ppermute x21, starting transfers between devices, extended(): lax.ppermute(lax.slice_in_dim(block, block.shape[dim] - width, None, axis...  53 us
    ppermute x21, starting transfers between devices, extended(): lax.ppermute(lax.slice_in_dim(block, 0, width, axis=dim), axis, backward)  47.5 us
    ppermute x4, waiting for transfers between devices, shards(): lax.ppermute(image_part, 'mem', [(dev, dev ^ hop) for dev in range(4)])  47.1 us
    all_to_all x1, starting transfers between devices, shards(): lax.all_to_all(send_cells.reshape(blocks, capacity), 'col', split_axis=0,...  13.1 us
  transfers between devices with their start and end apart: 49, of which 27 were waited for; matrix products, arithmetic and copies ran while one was open for 2% of the time, Pallas kernels for 0%

profile of v1, /device:TPU:1, one launch (start us, length us, event | category | flops | bytes accessed | tf_op | source)
XLA Modules:
  0.0 576.1 jit_solution(8875814908723273261)
XLA Ops:
  6.7 13.1 %all-to-all-start = ((s32[64,1,8]{2,1,0:T(1,128)}), s32[64,1,8]{2,1,0:T(1,128)S(1)}, u32[]{:S(2)}, u32[]{:S(2)}) async-start(s32[64,1,8]{2,1,0:T(1,128)} %bitcast.6), calls=%async_computation | async-start | bytes 65536 | tf_op jit(solution)/shard_map/all_to_all | solution.py:93
  22.0 7.1 %all-to-all-done = s32[64,1,8]{2,1,0:T(1,128)S(1)} async-done(((s32[64,1,8]{2,1,0:T(1,128)}), s32[64,1,8]{2,1,0:T(1,128)S(1)}, u32[]{:S(2)}, u32[]{:S(2)}) %all-to-all-start) | async-done | bytes 2080 | tf_op jit(solution)/shard_map/all_to_all | solution.py:93
  29.1 4.7 all-to-all-start.1
  36.0 7.2 %all-to-all-done.1 = f32[64,1,8]{2,1,0:T(1,128)S(1)} async-done(((f32[64,1,8]{2,1,0:T(1,128)}), f32[64,1,8]{2,1,0:T(1,128)S(1)}, u32[]{:S(2)}, u32[]{:S(2)}) %all-to-all-start.1) | async-done | bytes 2080 | tf_op jit(solution)/shard_map/all_to_all | solution.py:96
  43.2 4.7 all-to-all-start.2
  48.7 3.5 collective-permute-start
  54.2 3.2 collective-permute-done.2
  62.2 2.4 scatter_custom_fusion.3
  66.5 3.3 collective-permute-start.1
  71.9 2.9 collective-permute-done.3
  77.0 2.4 collective-permute-start.5
  79.4 2.6 collective-permute-done.5
  84.2 2.4 collective-permute-start.7
  86.6 2.8 collective-permute-done.7
  91.7 2.4 collective-permute-start.9
  94.1 4.8 collective-permute-done.9
  101.1 2.5 collective-permute-start.11
  103.7 3.6 collective-permute-done.11
  109.5 2.4 collective-permute-start.13
  111.9 3.8 collective-permute-done.13
  121.2 2.9 collective-permute-done.15
  129.0 3.5 collective-permute-done.17
  136.2 10.3 %collective-permute-done.18 = f32[4,256,128]{2,1,0:T(8,128)S(1)} collective-permute-done((f32[4,256,128]{2,1,0:T(8,128)S(1)}, f32[4,256,128]{2,1,0:T(8,128)S(1)}, u32[]{:S(2)}, u32[]{:S(2)}) %collective-permute-start.18) | collective-permute-done | bytes 524320 | tf_op jit(solution)/shard_map/ppermute | solution.py:143
  146.6 2.8 collective-permute-start.19
  149.4 11.4 %collective-permute-done.19 = f32[4,256,128]{2,1,0:T(8,128)S(1)} collective-permute-done((f32[4,256,128]{2,1,0:T(8,128)S(1)}, f32[4,256,128]{2,1,0:T(8,128)S(1)}, u32[]{:S(2)}, u32[]{:S(2)}) %collective-permute-start.19) | collective-permute-done | bytes 524320 | tf_op jit(solution)/shard_map/ppermute | solution.py:143
  163.4 2.8 scatter_custom_fusion.4
  166.2 2.4 fusion.6
  169.8 5.6 collective-permute-start.20
  177.4 3.0 collective-permute-done.21
  185.0 2.9 collective-permute-done.23
  192.5 4.2 collective-permute-done.25
  202.3 4.5 collective-permute-done.27
  210.2 86.9 %all-reduce.21 = (f32[]{:T(128)}, f32[]{:T(128)}) all-reduce(f32[]{:T(128)S(6)} %add.409, f32[]{:T(128)S(6)} %add.447), channel_id=1, replica_groups=mesh['mem'=4,'col'=64] {'mem','col'}, use_global_device_ids=true, to_apply=%region_9.10 | all-reduce | flops 2 | bytes 16 | tf_op jit(solution)/shard_map/psum | solution.py:128
  301.0 72.8 %psum.30 = f32[]{:T(128)} all-reduce(f32[]{:T(128)S(6)} %add.448), channel_id=1, replica_groups=mesh['mem'=4,'col'=64] {'mem','col'}, use_global_device_ids=true, to_apply=%region_16.17 | all-reduce | flops 1 | bytes 8 | tf_op jit(solution)/shard_map/psum | solution.py:154
  375.0 4.2 collective-permute-start.28
  381.2 3.0 collective-permute-done.29
  388.8 2.6 collective-permute-done.31
  396.0 2.6 collective-permute-done.33
  403.2 2.6 collective-permute-done.35
  410.9 11.7 %collective-permute-done.36 = f32[4,256,128]{2,1,0:T(8,128)S(1)} collective-permute-done((f32[4,256,128]{2,1,0:T(8,128)S(1)}, f32[4,256,128]{2,1,0:T(8,128)S(1)}, u32[]{:S(2)}, u32[]{:S(2)}) %collective-permute-start.36) | collective-permute-done | bytes 524320 | tf_op jit(solution)/shard_map/ppermute | solution.py:143
  424.4 13.7 %collective-permute-done.37 = f32[4,256,128]{2,1,0:T(8,128)S(1)} collective-permute-done((f32[4,256,128]{2,1,0:T(8,128)S(1)}, f32[4,256,128]{2,1,0:T(8,128)S(1)}, u32[]{:S(2)}, u32[]{:S(2)}) %collective-permute-start.37) | collective-permute-done | bytes 524320 | tf_op jit(solution)/shard_map/ppermute | solution.py:143
  443.2 3.5 scatter_custom_fusion.5
  447.8 2.4 fusion.2
  452.8 4.9 collective-permute-start.38
  459.7 3.0 collective-permute-done.39
  468.9 2.6 collective-permute-done.41
  476.1 2.6 collective-permute-done.43
  488.0 85.1 %psum.31 = f32[]{:T(128)} all-reduce(f32[]{:T(128)S(6)} %add.488), channel_id=1, replica_groups=mesh['mem'=4,'col'=64] {'mem','col'}, use_global_device_ids=true, to_apply=%region_20.21 | all-reduce | flops 1 | bytes 8 | tf_op jit(solution)/shard_map/psum | solution.py:152
  (194 shorter events, 121.8 us)
Async XLA Ops:
  6.7 22.4 %all-to-all-start = ((s32[64,1,8]{2,1,0:T(1,128)}), s32[64,1,8]{2,1,0:T(1,128)S(1)}, u32[]{:S(2)}, u32[]{:S(2)}) async-start(s32[64,1,8]{2,1,0:T(1,128)} %bitcast.6), calls=%async_computation | async-start | bytes 65536 | tf_op jit(solution)/shard_map/all_to_all | solution.py:93
  29.1 14.1 %all-to-all-start.1 = ((f32[64,1,8]{2,1,0:T(1,128)}), f32[64,1,8]{2,1,0:T(1,128)S(1)}, u32[]{:S(2)}, u32[]{:S(2)}) async-start(f32[64,1,8]{2,1,0:T(1,128)} %bitcast.8), calls=%async_computation.1 | async-start | bytes 65536 | tf_op jit(solution)/shard_map/all_to_all | solution.py:96
  43.2 17.7 %all-to-all-start.2 = ((f32[64,8,128]{2,1,0:T(8,128)}), f32[64,8,128]{2,1,0:T(8,128)S(1)}, u32[]{:S(2)}, u32[]{:S(2)}) async-start(f32[64,8,128]{2,1,0:T(8,128)} %bitcast.9), calls=%async_computation.2 | async-start | bytes 524288 | tf_op jit(solution)/shard_map/all_to_all | solution.py:86
  48.7 5.5 collective-permute-start
  52.2 5.2 collective-permute-start.2
  66.5 5.3 collective-permute-start.1
  69.9 5.0 collective-permute-start.3
  75.1 4.3 collective-permute-start.4
  77.0 5.0 collective-permute-start.5
  82.3 4.3 collective-permute-start.6
  84.2 5.2 collective-permute-start.7
  89.7 4.3 collective-permute-start.8
  91.7 7.2 %collective-permute-start.9 = (f32[8,1,256]{2,1,0:T(1,128)S(1)}, f32[8,1,256]{2,1,0:T(1,128)S(1)}, u32[]{:S(2)}, u32[]{:S(2)}) collective-permute-start(f32[8,1,256]{2,1,0:T(1,128)S(1)} %get-tuple-element.41), channel_id=1, source_target_pairs={{1,0},{2,1},{3,2},{4,3},{5,4},{6,5},{7,6},{8,7},{9,8},{10,9},{11,1... | collective-permute-start | bytes 24584 | tf_op jit(solution)/shard_map/ppermute | solution.py:18
  99.2 4.5 collective-permute-start.10
  101.1 6.2 %collective-permute-start.11 = (f32[8,1,256]{2,1,0:T(1,128)S(1)}, f32[8,1,256]{2,1,0:T(1,128)S(1)}, u32[]{:S(2)}, u32[]{:S(2)}) collective-permute-start(f32[8,1,256]{2,1,0:T(1,128)S(1)} %get-tuple-element.39), channel_id=1, source_target_pairs={{1,0},{2,1},{3,2},{4,3},{5,4},{6,5},{7,6},{8,7},{9,8},{10,9},{11,1... | collective-permute-start | bytes 24584 | tf_op jit(solution)/shard_map/ppermute | solution.py:18
  107.6 4.4 collective-permute-start.12
  109.5 6.2 %collective-permute-start.13 = (f32[8,1,256]{2,1,0:T(1,128)S(1)}, f32[8,1,256]{2,1,0:T(1,128)S(1)}, u32[]{:S(2)}, u32[]{:S(2)}) collective-permute-start(f32[8,1,256]{2,1,0:T(1,128)S(1)} %get-tuple-element.37), channel_id=1, source_target_pairs={{1,0},{2,1},{3,2},{4,3},{5,4},{6,5},{7,6},{8,7},{9,8},{10,9},{11,1... | collective-permute-start | bytes 24584 | tf_op jit(solution)/shard_map/ppermute | solution.py:18
  116.0 5.2 collective-permute-start.14
  117.9 6.2 %collective-permute-start.15 = (f32[8,1,256]{2,1,0:T(1,128)S(1)}, f32[8,1,256]{2,1,0:T(1,128)S(1)}, u32[]{:S(2)}, u32[]{:S(2)}) collective-permute-start(f32[8,1,256]{2,1,0:T(1,128)S(1)} %get-tuple-element.35), channel_id=1, source_target_pairs={{1,0},{2,1},{3,2},{4,3},{5,4},{6,5},{7,6},{8,7},{9,8},{10,9},{11,1... | collective-permute-start | bytes 24584 | tf_op jit(solution)/shard_map/ppermute | solution.py:18
  124.4 4.6 collective-permute-start.16
  126.3 6.2 %collective-permute-start.17 = (f32[8,1,256]{2,1,0:T(1,128)S(1)}, f32[8,1,256]{2,1,0:T(1,128)S(1)}, u32[]{:S(2)}, u32[]{:S(2)}) collective-permute-start(f32[8,1,256]{2,1,0:T(1,128)S(1)} %get-tuple-element.33), channel_id=1, source_target_pairs={{1,0},{2,1},{3,2},{4,3},{5,4},{6,5},{7,6},{8,7},{9,8},{10,9},{11,1... | collective-permute-start | bytes 24584 | tf_op jit(solution)/shard_map/ppermute | solution.py:18
  134.9 11.6 %collective-permute-start.18 = (f32[4,256,128]{2,1,0:T(8,128)S(1)}, f32[4,256,128]{2,1,0:T(8,128)S(1)}, u32[]{:S(2)}, u32[]{:S(2)}) collective-permute-start(f32[4,256,128]{2,1,0:T(8,128)S(1)} %add_dynamic-update-slice_fusion), channel_id=1, source_target_pairs={{0,64},{64,0},{128,192},{192,128},{1,65},{65,1},{129,193},{193,129... | collective-permute-start | bytes 1572872 | tf_op jit(solution)/shard_map/ppermute | solution.py:143
  146.6 14.2 %collective-permute-start.19 = (f32[4,256,128]{2,1,0:T(8,128)S(1)}, f32[4,256,128]{2,1,0:T(8,128)S(1)}, u32[]{:S(2)}, u32[]{:S(2)}) collective-permute-start(f32[4,256,128]{2,1,0:T(8,128)S(1)} %add.427), channel_id=1, source_target_pairs={{0,128},{64,192},{128,0},{192,64},{1,129},{65,193},{129,1},{193,65... | collective-permute-start | bytes 1572872 | tf_op jit(solution)/shard_map/ppermute | solution.py:143
  169.8 7.5 %collective-permute-start.20 = (f32[8,1,256]{2,1,0:T(1,128)S(1)}, f32[8,1,256]{2,1,0:T(1,128)S(1)}, u32[]{:S(2)}, u32[]{:S(2)}) collective-permute-start(f32[8,1,256]{2,1,0:T(1,128)S(1)} %get-tuple-element.30), channel_id=1, source_target_pairs={{0,1},{1,2},{2,3},{3,4},{4,5},{5,6},{6,7},{7,8},{8,9},{9,10},{10,1... | collective-permute-start | bytes 24584 | tf_op jit(solution)/shard_map/ppermute | solution.py:15
  175.4 5.0 collective-permute-start.21
  180.7 4.3 collective-permute-start.22
  182.6 5.3 collective-permute-start.23
  188.2 4.3 collective-permute-start.24
  190.5 6.3 %collective-permute-start.25 = (f32[8,1,256]{2,1,0:T(1,128)S(1)}, f32[8,1,256]{2,1,0:T(1,128)S(1)}, u32[]{:S(2)}, u32[]{:S(2)}) collective-permute-start(f32[8,1,256]{2,1,0:T(1,128)S(1)} %get-tuple-element.27), channel_id=1, source_target_pairs={{1,0},{2,1},{3,2},{4,3},{5,4},{6,5},{7,6},{8,7},{9,8},{10,9},{11,1... | collective-permute-start | bytes 24584 | tf_op jit(solution)/shard_map/ppermute | solution.py:18
  197.0 5.2 collective-permute-start.26
  199.0 7.8 %collective-permute-start.27 = (f32[8,1,256]{2,1,0:T(1,128)S(1)}, f32[8,1,256]{2,1,0:T(1,128)S(1)}, u32[]{:S(2)}, u32[]{:S(2)}) collective-permute-start(f32[8,1,256]{2,1,0:T(1,128)S(1)} %get-tuple-element.25), channel_id=1, source_target_pairs={{1,0},{2,1},{3,2},{4,3},{5,4},{6,5},{7,6},{8,7},{9,8},{10,9},{11,1... | collective-permute-start | bytes 24584 | tf_op jit(solution)/shard_map/ppermute | solution.py:18
  375.0 6.2 %collective-permute-start.28 = (f32[8,1,256]{2,1,0:T(1,128)S(1)}, f32[8,1,256]{2,1,0:T(1,128)S(1)}, u32[]{:S(2)}, u32[]{:S(2)}) collective-permute-start(f32[8,1,256]{2,1,0:T(1,128)S(1)} %get-tuple-element.22), channel_id=1, source_target_pairs={{0,1},{1,2},{2,3},{3,4},{4,5},{5,6},{6,7},{7,8},{8,9},{9,10},{10,1... | collective-permute-start | bytes 24584 | tf_op jit(solution)/shard_map/ppermute | solution.py:15
  379.3 5.0 collective-permute-start.29
  384.5 4.3 collective-permute-start.30
  386.5 5.0 collective-permute-start.31
  391.7 4.3 collective-permute-start.32
  393.6 5.0 collective-permute-start.33
  400.8 5.0 collective-permute-start.35
  409.9 12.8 %collective-permute-start.36 = (f32[4,256,128]{2,1,0:T(8,128)S(1)}, f32[4,256,128]{2,1,0:T(8,128)S(1)}, u32[]{:S(2)}, u32[]{:S(2)}) collective-permute-start(f32[4,256,128]{2,1,0:T(8,128)S(1)} %fusion.1), channel_id=1, source_target_pairs={{0,64},{64,0},{128,192},{192,128},{1,65},{65,1},{129,193},{193,129... | collective-permute-start | bytes 1572872 | tf_op jit(solution)/shard_map/ppermute | solution.py:143
  422.7 15.4 %collective-permute-start.37 = (f32[4,256,128]{2,1,0:T(8,128)S(1)}, f32[4,256,128]{2,1,0:T(8,128)S(1)}, u32[]{:S(2)}, u32[]{:S(2)}) collective-permute-start(f32[4,256,128]{2,1,0:T(8,128)S(1)} %add.468), channel_id=1, source_target_pairs={{0,128},{64,192},{128,0},{192,64},{1,129},{65,193},{129,1},{193,65... | collective-permute-start | bytes 1572872 | tf_op jit(solution)/shard_map/ppermute | solution.py:143
  452.8 6.9 %collective-permute-start.38 = (f32[8,1,256]{2,1,0:T(1,128)S(1)}, f32[8,1,256]{2,1,0:T(1,128)S(1)}, u32[]{:S(2)}, u32[]{:S(2)}) collective-permute-start(f32[8,1,256]{2,1,0:T(1,128)S(1)} %get-tuple-element.14), channel_id=1, source_target_pairs={{0,1},{1,2},{2,3},{3,4},{4,5},{5,6},{6,7},{7,8},{8,9},{9,10},{10,1... | collective-permute-start | bytes 24584 | tf_op jit(solution)/shard_map/ppermute | solution.py:15
  457.7 5.0 collective-permute-start.39
  464.6 4.3 collective-permute-start.40
  466.5 5.0 collective-permute-start.41
  471.8 4.3 collective-permute-start.42
  473.7 5.0 collective-permute-start.43
  479.0 6.1 %collective-permute-start.44 = (f32[8,1,256]{2,1,0:T(1,128)S(1)}, f32[8,1,256]{2,1,0:T(1,128)S(1)}, u32[]{:S(2)}, u32[]{:S(2)}) collective-permute-start(f32[8,1,256]{2,1,0:T(1,128)S(1)} %get-tuple-element.8), channel_id=1, source_target_pairs={{0,1},{1,2},{2,3},{3,4},{4,5},{5,6},{6,7},{7,8},{8,9},{9,10},{10,1... | collective-permute-start | bytes 24584 | tf_op jit(solution)/shard_map/ppermute | solution.py:15
  480.9 5.0 collective-permute-start.45
  (9 other events, 376.7 us)
